TPU v7x, 128 devices: a whole 4x4x4 slice. The times are simulated.
128 devices in a mesh: feed: 8 (over y, core), chan: 16 (over z, x).
Axes of the slice: x: 4, y: 4, z: 4, core: 2. Of those that a mesh axis runs over, the one named last changes fastest.
Arguments:
- voltages: bfloat16 [2, 2, 16, 8192, 1024], P(None, None, 'chan', None, 'feed'), may hold values from -6 to 6
- history: bfloat16 [2, 2, 16, 48, 1024], P(None, None, 'chan', None, 'feed'), may hold values from -6 to 6
- gains: float32 [2, 2, 16, 1024], P(None, None, 'chan', 'feed'), may hold values from -4 to 4
- weights: bfloat16 [2, 16, 1024, 1024], P(None, 'chan'), may hold values from -0.09375 to 0.09375
- beam_lists: int32 [16, 128], replicated, may hold values from 0 to 1023, as said below
- beam_counts: int32 [16], replicated, may hold values from 1 to 128, as said below
Outputs:
- power_blocks: bfloat16 [256, 256, 2048], P('feed', None, 'chan')
Inputs may be any that keep to these rules, and one draw needn't show every extreme that they name: `beam_lists`: row n holds in its first beam_counts[n] entries, in increasing order, the beams that node n owns, and 0 in the others; every beam is owned by exactly one node. `beam_counts`: the counts sum to 1024; some node owns exactly 128 beams.
All inputs are finite; a program needn't handle non-finite values.
Results may differ from a plain program's by a relative error of at most 0.013.
Values may be sent and summed in bfloat16 or wider, within the bound.
No kernel may reach another device: no remote copies, remote signals or barrier semaphores. Data moves between devices by JAX's collectives and lax.ppermute only.
A program may use at most 192 MiB of HBM per device.

v0:
```python
import math
import jax
import jax.numpy as jnp
from jax import lax
from jax.sharding import PartitionSpec as P

U = 16
TAPS = 4
TINT = 2


def window_taps():
    length = TAPS * U
    positions = jnp.arange(length, dtype=jnp.float32)
    offsets = (positions - (length - 1) / 2.0) / U
    hann_taper = 0.5 - 0.5 * jnp.cos(2.0 * math.pi * (positions + 0.5) / length)
    taps_window = jnp.sinc(offsets) * hann_taper
    return taps_window / jnp.sqrt(jnp.sum(taps_window * taps_window) / U)


def dft_table():
    index_n = jnp.arange(U, dtype=jnp.int32)
    products = index_n[:, None] * index_n[None, :] % U
    phases = 2.0 * math.pi * products.astype(jnp.float32) / U
    cosine = jnp.cos(phases) / math.sqrt(U)
    sine = jnp.sin(phases) / math.sqrt(U)
    return jnp.stack([jnp.stack([cosine, -sine]), jnp.stack([sine, cosine])])


def filterbank(stream, frames, gains):
    shape_in = stream.shape
    taps_window = window_taps().reshape(TAPS, U)
    table = dft_table()
    frames_data = stream.reshape(
        shape_in[0], shape_in[1], shape_in[2], frames + TAPS - 1, U, shape_in[4]
    )
    filtered = taps_window[0][:, None] * frames_data[:, :, :, 0:frames].astype(jnp.float32)
    for tap_index in range(1, TAPS):
        filtered = filtered + taps_window[tap_index][:, None] * frames_data[
            :, :, :, tap_index : tap_index + frames
        ].astype(jnp.float32)
    spec_parts = []
    for part_out in range(2):
        total = None
        for part_in in range(2):
            for index_n in range(U):
                term = (
                    filtered[part_in, :, :, :, index_n : index_n + 1, :]
                    * table[part_in, part_out, index_n][:, None]
                )
                total = term if total is None else total + term
        spec_parts.append(total)
    gain_cols = gains[:, :, :, None, None, :]
    real_part = gain_cols[0] * spec_parts[0] - gain_cols[1] * spec_parts[1]
    imag_part = gain_cols[0] * spec_parts[1] + gain_cols[1] * spec_parts[0]
    return jnp.stack([real_part, imag_part]).astype(jnp.bfloat16)


def detect(calibrated, weights):
    spectra_here = calibrated.shape[3]
    fine_items = calibrated.shape[4]
    beam_total = weights.shape[3]
    rows_real = calibrated[0, :, 0].reshape(-1, calibrated.shape[5])
    rows_imag = calibrated[1, :, 0].reshape(-1, calibrated.shape[5])
    weight_real = weights[0, 0]
    weight_imag = weights[1, 0]
    upper_block = jnp.concatenate([weight_real, weight_imag], axis=1)
    lower_block = jnp.concatenate([-weight_imag, weight_real], axis=1)
    joined = jnp.dot(rows_real, upper_block, preferred_element_type=jnp.float32) + jnp.dot(
        rows_imag, lower_block, preferred_element_type=jnp.float32
    )
    real_part = joined[:, :beam_total]
    imag_part = joined[:, beam_total:]
    power_sum = (real_part * real_part + imag_part * imag_part).reshape(
        2, spectra_here, fine_items, beam_total
    )
    power_sum = jnp.sum(power_sum, axis=0).reshape(
        spectra_here // TINT, TINT, fine_items, beam_total
    )
    power_sum = jnp.sum(power_sum, axis=1) * (1.0 / (4.0 * TINT))
    outputs = [power_sum.astype(jnp.bfloat16)]
    return jnp.stack(outputs, axis=1)


def on_device(voltages, history, gains, weights, beam_lists, beam_counts):
    capacity = beam_lists.shape[1]
    flat_ids = beam_lists.reshape(-1)
    live_slots = (jnp.arange(capacity, dtype=jnp.int32)[None, :] < beam_counts[:, None]).reshape(-1)
    stream = jnp.concatenate([history, voltages], axis=3)
    calibrated = filterbank(stream, voltages.shape[3] // U, gains)
    beam_calibrated = lax.all_to_all(calibrated, "feed", split_axis=3, concat_axis=5, tiled=True)
    detected = detect(beam_calibrated, weights)
    bins_local, coarse_local, fine_items, beam_total = detected.shape
    picked = jnp.take(
        detected.reshape(bins_local, coarse_local * fine_items, beam_total), flat_ids, axis=2
    )
    return lax.all_to_all(
        jnp.where(live_slots, picked, jnp.zeros((), jnp.bfloat16)),
        "chan",
        split_axis=2,
        concat_axis=1,
        tiled=True,
    )


def solution(mesh):
    in_specs = (
        P(None, None, "chan", None, "feed"),
        P(None, None, "chan", None, "feed"),
        P(None, None, "chan", "feed"),
        P(None, "chan", None, None),
        P(),
        P(),
    )
    out_specs = P("feed", None, "chan")
    return jax.shard_map(
        on_device, mesh=mesh, in_specs=in_specs, out_specs=out_specs, check_vma=False
    )
```

profile of v0, /device:TPU:0, one launch (start us, length us, event | category | flops | bytes accessed | tf_op | source)
XLA Modules:
  0.0 429.2 jit_solution(4782768966015367416)
XLA Ops:
  0.0 0.7 multiply_reduce_fusion
  0.7 4.3 pad_maximum_fusion
  5.0 11.6 %fusion.35 = (bf16[2,2,1,512,16,128]{5,4,3,1,0,2:T(8,128)(2,1)}, bf16[2,2,1,512,16,128]{5,4,3,1,0,2:T(8,128)(2,1)}, bf16[2,2,1,512,16,128]{5,4,3,1,0,2:T(8,128)(2,1)}, bf16[2,2,1,512,16,128]{5,4,3,1,0,2:T(8,128)(2,1)}) fusion(bf16[2,2,1,515,16,128]{5,4,3,1,0,2:T(8,128)(2,1)S(1)} %bitcast.249), kind=kLoop, calls=%fused_computation.172 | loop fusion | bytes 67108864 | tf_op jit(solution)/shard_map/slice | solution.py:37
  17.3 0.1 fusion.38
  17.4 56.0 %multiply_add_fusion = f32[2,2,1,512,16,128]{5,1,3,4,2,0:T(2,128)} fusion(f32[16]{0:T(128)S(1)} %get-tuple-element.117, f32[16]{0:T(128)S(1)} %get-tuple-element.118, f32[16]{0:T(128)S(1)} %get-tuple-element.119, f32[16]{0:T(128)S(1)} %get-tuple-element.116, bf16[2,2,1,512,16,128]{5,4,3,1,0,2:T(8,128)(2,1)} %get-tuple-element.43, ...), kind=kLoop, calls=%fused_computation.1 | loop fusion | flops 46137344 | bytes 50331904 | tf_op jit(solution)/shard_map/add | solution.py:39
  73.3 6.9 %slice_bitcast_fusion.33 = (f32[2,512,128]{2,0,1:T(2,128)S(1)}, f32[2,512,128]{2,0,1:T(2,128)S(1)}, f32[2,512,128]{2,0,1:T(2,128)S(1)}, f32[2,512,128]{2,0,1:T(2...) fusion(f32[2,2,1,512,16,128]{5,1,3,4,2,0:T(2,128)} %multiply_ad, ...), kind=kLoop, calls=%fused_computation.61 | loop fusion | bytes 19922944 | tf_op jit(solution)/shard_map/mul | solution.py:48
  80.2 4.9 %slice_bitcast_fusion.32 = (f32[2,512,128]{2,0,1:T(2,128)}, f32[2,512,128]{2,0,1:T(2,128)}, f32[2,512,128]{2,0,1:T(2,128)}, f32[2,512,128]{2,0,1:T(2,128)}, f32[...) fusion(f32[2,2,1,512,16,128]{5,1,3,4,2,0:T(2,128)} %multiply_ad, ...), kind=kLoop, calls=%fused_computation.60 | loop fusion | bytes 13631488 | tf_op jit(solution)/shard_map/mul | solution.py:48
  85.4 49.3 %fusion.1 = (bf16[1,2,1,512,16,128]{5,4,1,0,2,3:T(8,128)(2,1)}, f32[1,2,512,16,128]{4,3,1,2,0:T(8,128)}, f32[1,2,512,16,128]{4,3,1,2,0:T(8,128)}) fusion(f32[2,128]{1,0:T(2,128)S(1)} %bitcast.259, f32[2,128]{1,0:T(2,128)S(1)} %bitcast.257, f32[16]{0:T(128)S(1)} %get-tuple-element.81, f32[2,512,128]{2,0,1:T(2,128)S(1)} %get-tuple-element.9, ...), kind=kLoop, calls=%fused_computation.13 | loop fusion | flops 272629760 | bytes 37754880 | tf_op jit(solution)/shard_map/stack | solution.py:56
  134.7 7.9 %fusion.2 = bf16[1,2,1,512,16,128]{5,4,1,0,2,3:T(8,128)(2,1)S(1)} fusion(f32[1,2,512,16,128]{4,3,1,2,0:T(8,128)} %get-tuple-element.7, f32[1,2,512,16,128]{4,3,1,2,0:T(8,128)} %get-tuple-element.6, f32[2,128]{1,0:T(2,128)S(1)} %bitcast.260, f32[2,128]{1,0:T(2,128)S(1)} %bitcast.258), kind=kLoop, calls=%fused_computation.14 | loop fusion | flops 8388608 | bytes 20973568 | tf_op jit(solution)/shard_map/stack | solution.py:56
  142.6 6.5 %pad_maximum_fusion.1 = bf16[2,2,1,512,16,128]{5,4,1,0,2,3:T(8,128)(2,1)} fusion(bf16[1,2,1,512,16,128]{5,4,1,0,2,3:T(8,128)(2,1)S(1)} %fusion.2, bf16[1,2,1,512,16,128]{5,4,1,0,2,3:T(8,128)(2,1)} %get-tuple-element.5), kind=kLoop, calls=%fused_computation.6 | loop fusion | flops 4194304 | bytes 16777216 | tf_op jit(solution)/shard_map/stack | solution.py:56
  149.1 5.1 %all-to-all-start = ((bf16[2,2,1,512,16,128]{5,4,1,0,2,3:T(8,128)(2,1)}), bf16[2,2,1,512,16,128]{5,4,1,0,2,3:T(8,128)(2,1)}, u32[]{:S(2)}, u32[]{:S(2)}) async-start(bf16[2,2,1,512,16,128]{5,4,1,0,2,3:T(8,128)(2,1)} %pad_maximum_fusion.1), calls=%async_computation | async-start | bytes 16777216 | tf_op jit(solution)/shard_map/all_to_all | solution.py:91
  154.2 0.1 fusion.20
  154.3 1.7 fusion.34
  156.0 4.7 %slice_bitcast_fusion.1 = (bf16[1024,1024]{1,0:T(8,128)(2,1)}, bf16[1024,1024]{1,0:T(8,128)(2,1)}) fusion(bf16[2,1,1024,1024]{3,2,1,0:T(8,128)(2,1)} %param.9), kind=kLoop, calls=%fused_computation.29 | loop fusion | bytes 8388608 | tf_op jit(solution)/shard_map/squeeze | solution.py:65
  160.7 88.1 %all-to-all-done = bf16[2,2,1,512,16,128]{5,4,1,0,2,3:T(8,128)(2,1)} async-done(((bf16[2,2,1,512,16,128]{5,4,1,0,2,3:T(8,128)(2,1)}), bf16[2,2,1,512,16,128]{5,4,1,0,2,3:T(8,128)(2,1)}, u32[]{:S(2)}, u32[]{:S(2)}) %all-to-all-start) | async-done | bytes 8388640 | tf_op jit(solution)/shard_map/all_to_all | solution.py:91
  248.8 8.1 %copy.43 = bf16[2,2,1,512,16,128]{5,4,3,1,0,2:T(8,128)(2,1)} copy(bf16[2,2,1,512,16,128]{5,4,1,0,2,3:T(8,128)(2,1)} %all-to-all-done) | data formatting | bytes 16777216 | tf_op jit(solution)/shard_map/all_to_all | solution.py:91
  256.8 4.4 %fusion.36 = (bf16[1,2,1,64,16,8,128]{6,4,3,5,1,0,2:T(8,128)(2,1)S(1)}, bf16[1,2,1,64,16,8,128]{6,4,3,5,1,0,2:T(8,128)(2,1)S(1)}) fusion(bf16[2,2,1,64,16,8,128]{6,4,3,5,1,0,2:T(8,128)(2,1)} %bitcast.252), kind=kLoop, calls=%fused_computation.173 | loop fusion | bytes 16777216 | tf_op jit(solution)/shard_map/slice | solution.py:64
  261.2 4.9 %copy.44 = bf16[1,2,1,64,16,8,128]{6,5,4,3,1,2,0:T(8,128)(2,1)S(1)} copy(bf16[1,2,1,64,16,8,128]{6,4,3,5,1,0,2:T(8,128)(2,1)S(1)} %get-tuple-element.45) | data formatting | bytes 8388608 | tf_op jit(solution)/shard_map/slice | solution.py:63
  266.1 4.9 %copy.45 = bf16[1,2,1,64,16,8,128]{6,5,4,3,1,2,0:T(8,128)(2,1)S(1)} copy(bf16[1,2,1,64,16,8,128]{6,4,3,5,1,0,2:T(8,128)(2,1)S(1)} %get-tuple-element.44) | data formatting | bytes 8388608 | tf_op jit(solution)/shard_map/slice | solution.py:64
  271.0 12.0 %fusion.5 = f32[2048,2048]{1,0:T(8,128)} fusion(bf16[256,8,8,128]{3,2,1,0:T(8,128)(2,1)S(1)} %bitcast.254, bf16[1024,1024]{1,0:T(8,128)(2,1)S(1)} %copy-done.1, bf16[1024,1024]{1,0:T(8,128)(2,1)S(1)} %copy-done), kind=kOutput, calls=%fused_computation.17 | convolution fusion | flops 8598323200 | bytes 25165824 | tf_op jit(solution)/shard_map/dot_general | solution.py:69
  282.9 17.8 %convolution_add_fusion = f32[2048,2048]{1,0:T(8,128)} fusion(f32[2048,2048]{1,0:T(8,128)} %fusion.5, bf16[256,8,8,128]{3,2,1,0:T(8,128)(2,1)S(1)} %bitcast.253, bf16[1024,1024]{1,0:T(8,128)(2,1)} %get-tuple-element.46, bf16[1024,1024]{1,0:T(8,128)(2,1)S(1)} %fusion.34), kind=kOutput, calls=%fused_computation.12 | convolution fusion | flops 8602517504 | bytes 41943040 | tf_op jit(solution)/shard_map/dot_general | solution.py:69
  300.7 9.3 %fusion = f32[2048,1024]{1,0:T(8,128)} fusion(f32[2048,2048]{1,0:T(8,128)} %convolution_add_fusion), kind=kLoop, calls=%fused_computation.4 | loop fusion | flops 6291456 | bytes 25165824 | tf_op jit(solution)/shard_map/add | solution.py:74
  310.0 6.7 %reduce_sum.28 = f32[64,16,1024]{2,1,0:T(8,128)} reduce(f32[2,64,16,1024]{3,2,1,0:T(8,128)} %bitcast.250, f32[]{:T(128)} %constant.78.clone.1), dimensions={0}, to_apply=%region_1.2 | reduce | flops 1048576 | bytes 12582916 | tf_op jit(solution)/shard_map/reduce_sum | solution.py:77
  316.6 2.8 bitcast_reduce_fusion
  319.4 0.2 multiply_convert_fusion
  319.7 5.1 %copy.46 = bf16[32,16,1024]{0,1,2:T(8,128)(2,1)} copy(bf16[32,16,1024]{2,1,0:T(8,128)(2,1)S(1)} %multiply_convert_fusion) | data formatting | bytes 2097152 | tf_op jit(solution)/shard_map/convert_element_type | solution.py:81
  324.8 18.4 %gather_fusion = bf16[2048,32,16]{1,2,0:T(8,128)(2,1)} fusion(bf16[32,16,1024]{0,1,2:T(8,128)(2,1)} %copy.46, s32[2048]{0:T(1024)S(1)} %broadcast_clamp_fusion), kind=kCustom, calls=%fused_computation | custom fusion | bytes 4202496 | tf_op jit(solution)/shard_map/jit(_take)/gather | solution.py:94
  343.3 12.1 %fusion.39 = bf16[2048,16,32]{2,1,0:T(8,128)(2,1)} fusion(bf16[2048,32,16]{1,2,0:T(8,128)(2,1)} %gather_fusion, pred[2048]{0:T(1024)(128)(4,1)S(1)} %compare_and_fusion, pred[2048]{0:T(1024)(128)(4,1)S(1)} %fusion.20), kind=kLoop, calls=%fused_computation.176 | loop fusion | flops 2097152 | bytes 4198400
  355.3 13.4 %reshape.1023 = bf16[16,2,32768]{2,1,0:T(2,128)(2,1)S(1)} reshape(bf16[2048,16,32]{2,1,0:T(8,128)(2,1)} %fusion.39) | data formatting | bytes 4194304
  368.8 36.1 %all_to_all.33 = bf16[16,2,32768]{2,1,0:T(2,128)(2,1)} all-to-all(bf16[16,2,32768]{2,1,0:T(2,128)(2,1)S(1)} %reshape.1023), channel_id=1, replica_groups=mesh['feed'=8,'chan'=16] {'chan'}, dimensions={0} | all-to-all | bytes 4194304 | tf_op jit(solution)/shard_map/all_to_all | solution.py:97
  404.8 12.9 %reshape.1024 = bf16[2048,16,32]{2,1,0:T(8,128)(2,1)} reshape(bf16[16,2,32768]{2,1,0:T(2,128)(2,1)} %all_to_all.33) | data formatting | bytes 4194304
  417.8 11.2 %copy.48 = bf16[32,16,16,128]{3,2,1,0:T(8,128)(2,1)} copy(bf16[32,16,16,128]{0,2,3,1:T(8,128)(2,1)} %bitcast.251) | data formatting | bytes 4194304 | tf_op jit(solution)/shard_map/all_to_all | solution.py:97
  (22 shorter events, 0.3 us)
Async XLA Ops:
  80.2 5.2 %copy-start.3 = (f32[2,2,1,128]{3,2,1,0:T(1,128)S(1)}, f32[2,2,1,128]{3,2,1,0:T(1,128)}, u32[]{:S(2)}) copy-start(f32[2,2,1,128]{3,2,1,0:T(1,128)} %param.8) | copy-start | bytes 6148
  149.1 5.1 %copy-start.4 = (s32[16]{0:T(128)S(1)}, s32[16]{0:T(128)}, u32[]{:S(2)}) copy-start(s32[16]{0:T(128)} %param.11) | copy-start | bytes 196
  149.1 5.2 %copy-start.2 = (s32[16,128]{1,0:T(8,128)S(1)}, s32[16,128]{1,0:T(8,128)}, u32[]{:S(2)}) copy-start(s32[16,128]{1,0:T(8,128)} %param.10) | copy-start | bytes 24580
  149.1 99.7 %all-to-all-start = ((bf16[2,2,1,512,16,128]{5,4,1,0,2,3:T(8,128)(2,1)}), bf16[2,2,1,512,16,128]{5,4,1,0,2,3:T(8,128)(2,1)}, u32[]{:S(2)}, u32[]{:S(2)}) async-start(bf16[2,2,1,512,16,128]{5,4,1,0,2,3:T(8,128)(2,1)} %pad_maximum_fusion.1), calls=%async_computation | async-start | bytes 16777216 | tf_op jit(solution)/shard_map/all_to_all | solution.py:91
  261.2 9.8 %copy-start = (bf16[1024,1024]{1,0:T(8,128)(2,1)S(1)}, bf16[1024,1024]{1,0:T(8,128)(2,1)}, u32[]{:S(2)}) copy-start(bf16[1024,1024]{1,0:T(8,128)(2,1)} %get-tuple-element.46) | copy-start | bytes 6291460
  261.2 9.7 %copy-start.1 = (bf16[1024,1024]{1,0:T(8,128)(2,1)S(1)}, bf16[1024,1024]{1,0:T(8,128)(2,1)}, u32[]{:S(2)}) copy-start(bf16[1024,1024]{1,0:T(8,128)(2,1)} %get-tuple-element.47) | copy-start | bytes 6291460
where the time goes:
time: 438 us; the launch traced here: 429 us
  other arithmetic  158 us (36%)
  local copies, waits for them, and re-layouts  111 us (25%)
  waiting for transfers between devices  88.1 us (20%)
  blocking collectives  36.1 us (8%)
  matrix products  29.7 us (7%)
  starting transfers between devices  5.08 us (1%)
    all_to_all x1, waiting for transfers between devices, on_device(): lax.all_to_all(calibrated, 'feed', split_axis=3, concat_axis=5, tiled=True)  88.1 us
    another operation x3, other arithmetic, filterbank(): return jnp.stack([real_part, imag_part]).astype(jnp.bfloat16)  63.7 us
    add x1, other arithmetic, filterbank(): filtered + taps_window[tap_index][:, None] * frames_data[:, :, :, tap_ind...  56 us
    all_to_all x1, blocking collectives, on_device(): lax.all_to_all(jnp.where(live_slots, picked, jnp.zeros((), jnp.bfloat16))...  36.1 us
    unnamed x12, local copies, waits for them, and re-layouts  26.4 us
    gather x1, local copies, waits for them, and re-layouts, on_device(): jnp.take(detected.reshape(bins_local, coarse_local * fine_items, beam_tot...  18.4 us
    dot_general x1, matrix products, detect(): jnp.dot(rows_imag, lower_block, preferred_element_type=jnp.float32)  17.8 us
    unnamed x1, other arithmetic  12.1 us
  transfers between devices with their start and end apart: 1, of which 1 were waited for; matrix products, arithmetic and copies ran while one was open for 2% of the time, Pallas kernels for 0%

commit v1 on v0

--- a/solution.py
+++ b/solution.py
@@ -88,7 +88,12 @@
     live_slots = (jnp.arange(capacity, dtype=jnp.int32)[None, :] < beam_counts[:, None]).reshape(-1)
     stream = jnp.concatenate([history, voltages], axis=3)
     calibrated = filterbank(stream, voltages.shape[3] // U, gains)
-    beam_calibrated = lax.all_to_all(calibrated, "feed", split_axis=3, concat_axis=5, tiled=True)
+    beam_calibrated = jnp.concatenate(
+        lax.all_to_all(
+            jnp.stack(jnp.split(calibrated, lax.axis_size("feed"), axis=3)), "feed", 0, 0
+        ),
+        axis=5,
+    )
     detected = detect(beam_calibrated, weights)
     bins_local, coarse_local, fine_items, beam_total = detected.shape
     picked = jnp.take(

time: 438 us -> 389 us (0.89); the launches traced: 429 us -> 387 us
  other arithmetic: 158 us -> 123 us
  local copies, waits for them, and re-layouts: 111 us -> 104 us
    add x1, other arithmetic: 56 us -> 18.8 us  [filterbank(): filtered + taps_window[tap_index][:, None] * frames_data[:, :, :, tap_ind...]
    unnamed x1 -> x8, other arithmetic: 12.1 us -> 21.5 us
    all_to_all x1 -> x0, local copies, waits for them, and re-layouts: 8.05 us -> none  [on_device(): lax.all_to_all(calibrated, 'feed', split_axis=3, concat_axis=5, tiled=True)]
    another operation x3 -> x2, other arithmetic: 63.7 us -> 55.9 us  [filterbank(): return jnp.stack([real_part, imag_part]).astype(jnp.bfloat16)]
    unnamed x12 -> x16, local copies, waits for them, and re-layouts: 26.4 us -> 26.4 us
where the time goes in v1:
time: 389 us; the launch traced here: 387 us
  other arithmetic  123 us (32%)
  local copies, waits for them, and re-layouts  104 us (27%)
  waiting for transfers between devices  88.1 us (23%)
  blocking collectives  36.1 us (9%)
  matrix products  29.7 us (8%)
  starting transfers between devices  5.27 us (1%)
    all_to_all x1, waiting for transfers between devices, on_device(): lax.all_to_all(jnp.stack(jnp.split(calibrated, lax.axis_size('feed'), axi...  88.1 us
    another operation x2, other arithmetic, filterbank(): return jnp.stack([real_part, imag_part]).astype(jnp.bfloat16)  55.9 us
    all_to_all x1, blocking collectives, on_device(): lax.all_to_all(jnp.where(live_slots, picked, jnp.zeros((), jnp.bfloat16))...  36.1 us
    unnamed x16, local copies, waits for them, and re-layouts  26.4 us
    unnamed x8, other arithmetic  21.5 us
    add x1, other arithmetic, filterbank(): filtered + taps_window[tap_index][:, None] * frames_data[:, :, :, tap_ind...  18.8 us
    gather x1, local copies, waits for them, and re-layouts, on_device(): jnp.take(detected.reshape(bins_local, coarse_local * fine_items, beam_tot...  18.4 us
    dot_general x1, matrix products, detect(): jnp.dot(rows_imag, lower_block, preferred_element_type=jnp.float32)  17.8 us
  transfers between devices with their start and end apart: 1, of which 1 were waited for; matrix products, arithmetic and copies ran while one was open for 2% of the time, Pallas kernels for 0%

profile of v1, /device:TPU:0, one launch (start us, length us, event | category | flops | bytes accessed | tf_op | source)
XLA Modules:
  0.0 387.3 jit_solution(10271877423435277908)
XLA Ops:
  0.7 4.3 %pad_maximum_fusion = bf16[2,2,1,8240,128]{4,3,2,1,0:T(8,128)(2,1)S(1)} fusion(bf16[2,2,1,8192,128]{4,3,2,1,0:T(8,128)(2,1)} %param.6, bf16[2,2,1,48,128]{4,3,2,1,0:T(8,128)(2,1)} %param.7), kind=kLoop, calls=%fused_computation.16 | loop fusion | flops 16875520 | bytes 16875520 | tf_op jit(solution)/shard_map/concatenate | solution.py:89
  5.0 11.6 %fusion.44 = (bf16[2,2,1,512,16,128]{5,4,3,1,0,2:T(8,128)(2,1)}, bf16[2,2,1,512,16,128]{5,4,3,1,0,2:T(8,128)(2,1)}, bf16[2,2,1,512,16,128]{5,4,3,1,0,2:T(8,128)(2,1)}, bf16[2,2,1,512,16,128]{5,4,3,1,0,2:T(8,128)(2,1)}) fusion(bf16[2,2,1,515,16,128]{5,4,3,1,0,2:T(8,128)(2,1)S(1)} %bitcast.265), kind=kLoop, calls=%fused_computation.202 | loop fusion | bytes 67108864 | tf_op jit(solution)/shard_map/slice | solution.py:37
  17.4 18.8 %multiply_add_fusion = f32[2,2,1,512,16,128]{5,3,1,4,2,0:T(8,128)} fusion(bf16[2,2,1,512,16,128]{5,4,3,1,0,2:T(8,128)(2,1)} %get-tuple-element.43, bf16[2,2,1,512,16,128]{5,4,3,1,0,2:T(8,128)(2,1)} %get-tuple-element.41, bf16[2,2,1,512,16,128]{5,4,3,1,0,2:T(8,128)(2,1)} %get-tuple-element.42, bf16[2,2,1,512,16,128]{5,4,3,1,0,2:T(8,128)(2,1)} %get-tuple-element.40, ...), kind=kLoop, calls=%fused_computation.1 | loop fusion | flops 46137344 | bytes 50331904 | tf_op jit(solution)/shard_map/add | solution.py:39
  36.2 6.7 %slice_bitcast_fusion.33 = (f32[2,512,128]{2,1,0:T(8,128)S(1)}, f32[2,512,128]{2,1,0:T(8,128)S(1)}, f32[2,512,128]{2,1,0:T(8,128)S(1)}, f32[2,512,128]{2,1,0:T(8...) fusion(f32[2,2,1,512,16,128]{5,3,1,4,2,0:T(8,128)} %multiply_ad, ...), kind=kLoop, calls=%fused_computation.91 | loop fusion | bytes 19922944 | tf_op jit(solution)/shard_map/mul | solution.py:48
  42.9 5.8 %slice_bitcast_fusion.32 = (f32[2,512,128]{2,1,0:T(8,128)}, f32[2,512,128]{2,1,0:T(8,128)}, f32[2,512,128]{2,1,0:T(8,128)}, f32[2,512,128]{2,1,0:T(8,128)}, f32[...) fusion(f32[2,2,1,512,16,128]{5,3,1,4,2,0:T(8,128)} %multiply_ad, ...), kind=kLoop, calls=%fused_computation.90 | loop fusion | bytes 13631488 | tf_op jit(solution)/shard_map/mul | solution.py:48
  48.9 46.9 %fusion.1 = (bf16[1,2,1,512,16,128]{5,4,3,1,0,2:T(8,128)(2,1)}, f32[1,2,512,16,128]{4,3,2,1,0:T(8,128)}, f32[1,2,512,16,128]{4,3,2,1,0:T(8,128)}) fusion(f32[2,128]{1,0:T(2,128)S(1)} %bitcast.274, f32[2,128]{1,0:T(2,128)S(1)} %bitcast.272, f32[16]{0:T(128)S(1)} %get-tuple-element.81, f32[2,512,128]{2,1,0:T(8,128)S(1)} %get-tuple-element.9, ...), kind=kLoop, calls=%fused_computation.26 | loop fusion | flops 272629760 | bytes 37754880 | tf_op jit(solution)/shard_map/stack | solution.py:56
  95.8 9.0 %fusion.2 = bf16[1,2,1,512,16,128]{5,4,3,1,0,2:T(8,128)(2,1)} fusion(f32[1,2,512,16,128]{4,3,2,1,0:T(8,128)} %get-tuple-element.7, f32[1,2,512,16,128]{4,3,2,1,0:T(8,128)} %get-tuple-element.6, f32[2,128]{1,0:T(2,128)S(1)} %bitcast.275, f32[2,128]{1,0:T(2,128)S(1)} %bitcast.273), kind=kLoop, calls=%fused_computation.27 | loop fusion | flops 8388608 | bytes 20973568 | tf_op jit(solution)/shard_map/stack | solution.py:56
  104.8 2.4 bitcast_dynamic-update-slice_fusion.6
  108.4 1.2 bitcast_dynamic-update-slice_fusion.4
  109.5 1.2 bitcast_dynamic-update-slice_fusion.3
  110.7 1.2 bitcast_dynamic-update-slice_fusion.2
  112.0 1.2 bitcast_dynamic-update-slice_fusion.1
  113.1 1.2 bitcast_dynamic-update-slice_fusion
  115.4 5.3 %all-to-all-start = ((bf16[8,2,2,1,64,16,128]{6,5,4,2,1,3,0:T(8,128)(2,1)}), bf16[8,2,2,1,64,16,128]{6,5,4,2,1,3,0:T(8,128)(2,1)}, u32[]{:S(2)}, u32[]{:S(2)}) async-start(bf16[8,2,2,1,64,16,128]{6,5,4,2,1,3,0:T(8,128)(2,1)} %fusion.22), calls=%async_computation | async-start | bytes 16777216 | tf_op jit(solution)/shard_map/all_to_all | solution.py:92
  120.8 1.7 fusion.43
  122.6 4.7 %slice_bitcast_fusion.1 = (bf16[1024,1024]{1,0:T(8,128)(2,1)}, bf16[1024,1024]{1,0:T(8,128)(2,1)}) fusion(bf16[2,1,1024,1024]{3,2,1,0:T(8,128)(2,1)} %param.9), kind=kLoop, calls=%fused_computation.42 | loop fusion | bytes 8388608 | tf_op jit(solution)/shard_map/squeeze | solution.py:65
  127.3 88.1 %all-to-all-done = bf16[8,2,2,1,64,16,128]{6,5,4,2,1,3,0:T(8,128)(2,1)} async-done(((bf16[8,2,2,1,64,16,128]{6,5,4,2,1,3,0:T(8,128)(2,1)}), bf16[8,2,2,1,64,16,128]{6,5,4,2,1,3,0:T(8,128)(2,1)}, u32[]{:S(2)}, u32[]{:S(2)}) %all-to-all-start) | async-done | bytes 8388640 | tf_op jit(solution)/shard_map/all_to_all | solution.py:92
  215.3 4.3 %fusion.45 = (bf16[1,2,1,64,16,8,128]{6,4,3,1,0,2,5:T(8,128)(2,1)S(1)}, bf16[1,2,1,64,16,8,128]{6,4,3,1,0,2,5:T(8,128)(2,1)S(1)}) fusion(bf16[2,2,1,64,16,8,128]{6,4,3,1,0,2,5:T(8,128)(2,1)} %bitcast.114), kind=kLoop, calls=%fused_computation.203 | loop fusion | bytes 16777216 | tf_op jit(solution)/shard_map/slice | solution.py:64
  219.6 4.9 %copy.47 = bf16[1,2,1,64,16,8,128]{6,5,4,3,1,2,0:T(8,128)(2,1)S(1)} copy(bf16[1,2,1,64,16,8,128]{6,4,3,1,0,2,5:T(8,128)(2,1)S(1)} %get-tuple-element.45) | data formatting | bytes 8388608 | tf_op jit(solution)/shard_map/slice | solution.py:63
  224.5 4.9 %copy.48 = bf16[1,2,1,64,16,8,128]{6,5,4,3,1,2,0:T(8,128)(2,1)S(1)} copy(bf16[1,2,1,64,16,8,128]{6,4,3,1,0,2,5:T(8,128)(2,1)S(1)} %get-tuple-element.44) | data formatting | bytes 8388608 | tf_op jit(solution)/shard_map/slice | solution.py:64
  229.4 12.0 %fusion.5 = f32[2048,2048]{1,0:T(8,128)} fusion(bf16[256,8,8,128]{3,2,1,0:T(8,128)(2,1)S(1)} %bitcast.269, bf16[1024,1024]{1,0:T(8,128)(2,1)S(1)} %copy-done.3, bf16[1024,1024]{1,0:T(8,128)(2,1)S(1)} %copy-done.2), kind=kOutput, calls=%fused_computation.30 | convolution fusion | flops 8598323200 | bytes 25165824 | tf_op jit(solution)/shard_map/dot_general | solution.py:69
  241.3 17.8 %convolution_add_fusion = f32[2048,2048]{1,0:T(8,128)} fusion(f32[2048,2048]{1,0:T(8,128)} %fusion.5, bf16[256,8,8,128]{3,2,1,0:T(8,128)(2,1)S(1)} %bitcast.268, bf16[1024,1024]{1,0:T(8,128)(2,1)} %get-tuple-element.46, bf16[1024,1024]{1,0:T(8,128)(2,1)S(1)} %fusion.43), kind=kOutput, calls=%fused_computation.25 | convolution fusion | flops 8602517504 | bytes 41943040 | tf_op jit(solution)/shard_map/dot_general | solution.py:69
  259.1 9.3 %fusion = f32[2048,1024]{1,0:T(8,128)} fusion(f32[2048,2048]{1,0:T(8,128)} %convolution_add_fusion), kind=kLoop, calls=%fused_computation.18 | loop fusion | flops 6291456 | bytes 25165824 | tf_op jit(solution)/shard_map/add | solution.py:74
  268.4 6.7 %reduce_sum.28 = f32[64,16,1024]{2,1,0:T(8,128)} reduce(f32[2,64,16,1024]{3,2,1,0:T(8,128)} %bitcast.266, f32[]{:T(128)} %constant.78.clone.1), dimensions={0}, to_apply=%region_1.2 | reduce | flops 1048576 | bytes 12582916 | tf_op jit(solution)/shard_map/reduce_sum | solution.py:77
  275.0 2.8 bitcast_reduce_fusion
  278.1 5.2 %copy.49 = bf16[32,16,1024]{0,1,2:T(8,128)(2,1)} copy(bf16[32,16,1024]{2,1,0:T(8,128)(2,1)S(1)} %multiply_convert_fusion) | data formatting | bytes 2097152 | tf_op jit(solution)/shard_map/convert_element_type | solution.py:81
  283.3 18.4 %gather_fusion = bf16[2048,32,16]{1,2,0:T(8,128)(2,1)} fusion(bf16[32,16,1024]{0,1,2:T(8,128)(2,1)} %copy.49, s32[2048]{0:T(1024)S(1)} %broadcast_clamp_fusion), kind=kCustom, calls=%fused_computation | custom fusion | bytes 4202496 | tf_op jit(solution)/shard_map/jit(_take)/gather | solution.py:99
  301.6 12.1 %fusion.48 = bf16[2048,16,32]{2,1,0:T(8,128)(2,1)} fusion(bf16[2048,32,16]{1,2,0:T(8,128)(2,1)} %gather_fusion, pred[2048]{0:T(1024)(128)(4,1)S(1)} %compare_and_fusion, pred[2048]{0:T(1024)(128)(4,1)S(1)} %fusion.29), kind=kLoop, calls=%fused_computation.206 | loop fusion | flops 2097152 | bytes 4198400
  313.7 13.4 %reshape.1028 = bf16[16,2,32768]{2,1,0:T(2,128)(2,1)S(1)} reshape(bf16[2048,16,32]{2,1,0:T(8,128)(2,1)} %fusion.48) | data formatting | bytes 4194304
  327.1 36.1 %all_to_all.23 = bf16[16,2,32768]{2,1,0:T(2,128)(2,1)} all-to-all(bf16[16,2,32768]{2,1,0:T(2,128)(2,1)S(1)} %reshape.1028), channel_id=1, replica_groups=mesh['feed'=8,'chan'=16] {'chan'}, dimensions={0} | all-to-all | bytes 4194304 | tf_op jit(solution)/shard_map/all_to_all | solution.py:102
  363.2 12.9 %reshape.1029 = bf16[2048,16,32]{2,1,0:T(8,128)(2,1)} reshape(bf16[16,2,32768]{2,1,0:T(2,128)(2,1)} %all_to_all.23) | data formatting | bytes 4194304
  376.1 11.2 %copy.51 = bf16[32,16,16,128]{3,2,1,0:T(8,128)(2,1)} copy(bf16[32,16,16,128]{0,2,3,1:T(8,128)(2,1)} %bitcast.267) | data formatting | bytes 4194304 | tf_op jit(solution)/shard_map/all_to_all | solution.py:102
  (32 shorter events, 3.6 us)
Async XLA Ops:
  42.9 6.0 %copy-start.5 = (f32[2,2,1,128]{3,2,1,0:T(1,128)S(1)}, f32[2,2,1,128]{3,2,1,0:T(1,128)}, u32[]{:S(2)}) copy-start(f32[2,2,1,128]{3,2,1,0:T(1,128)} %param.8) | copy-start | bytes 6148
  95.7 9.1 %copy-start = (bf16[1,2,1,512,16,128]{5,4,3,1,0,2:T(8,128)(2,1)S(1)}, bf16[1,2,1,512,16,128]{5,4,3,1,0,2:T(8,128)(2,1)}, u32[]{:S(2)}) copy-start(bf16[1,2,1,512,16,128]{5,4,3,1,0,2:T(8,128)(2,1)} %get-tuple-element.5) | copy-start | bytes 12582916
  104.8 2.4 copy-start.1
  115.4 5.3 %copy-start.6 = (s32[16]{0:T(128)S(1)}, s32[16]{0:T(128)}, u32[]{:S(2)}) copy-start(s32[16]{0:T(128)} %param.11) | copy-start | bytes 196
  115.4 5.4 %copy-start.4 = (s32[16,128]{1,0:T(8,128)S(1)}, s32[16,128]{1,0:T(8,128)}, u32[]{:S(2)}) copy-start(s32[16,128]{1,0:T(8,128)} %param.10) | copy-start | bytes 24580
  115.4 99.9 %all-to-all-start = ((bf16[8,2,2,1,64,16,128]{6,5,4,2,1,3,0:T(8,128)(2,1)}), bf16[8,2,2,1,64,16,128]{6,5,4,2,1,3,0:T(8,128)(2,1)}, u32[]{:S(2)}, u32[]{:S(2)}) async-start(bf16[8,2,2,1,64,16,128]{6,5,4,2,1,3,0:T(8,128)(2,1)} %fusion.22), calls=%async_computation | async-start | bytes 16777216 | tf_op jit(solution)/shard_map/all_to_all | solution.py:92
  219.6 9.8 %copy-start.2 = (bf16[1024,1024]{1,0:T(8,128)(2,1)S(1)}, bf16[1024,1024]{1,0:T(8,128)(2,1)}, u32[]{:S(2)}) copy-start(bf16[1024,1024]{1,0:T(8,128)(2,1)} %get-tuple-element.46) | copy-start | bytes 6291460
  219.6 9.7 %copy-start.3 = (bf16[1024,1024]{1,0:T(8,128)(2,1)S(1)}, bf16[1024,1024]{1,0:T(8,128)(2,1)}, u32[]{:S(2)}) copy-start(bf16[1024,1024]{1,0:T(8,128)(2,1)} %get-tuple-element.47) | copy-start | bytes 6291460
